TPU v7x, 32 devices: a whole 2x2x4 slice. The times are simulated.
32 devices in a mesh: section: 4 (over y, core), seq: 8 (over z, x).
Axes of the slice: x: 2, y: 2, z: 4, core: 2. Of those that a mesh axis runs over, the one named last changes fastest.
Arguments:
- queries: bfloat16 [4, 2048, 4096], P('section', 'seq'), may hold values from -42 to 42
- keys: bfloat16 [4, 2048, 512], P('section', 'seq'), may hold values from -6 to 6
- values: bfloat16 [4, 2048, 512], P('section', 'seq'), may hold values from -6 to 6
- out_grads: bfloat16 [4, 2048, 4096], P('section', 'seq'), may hold values from -6 to 6
- random_blocks: int32 [4, 32, 3], P('section'), may hold values from 0 to 31, as said below
- global_blocks: int32 [4, 2], P('section'), may hold values from 0 to 31, as said below
- pad_lengths: int32 [4, 8], P('section'), may hold values from 0 to 63, as said below
Outputs:
- passed_query_grad: bfloat16 [4, 2048, 4096], P('section', 'seq')
- passed_key_grad: bfloat16 [4, 2048, 512], P('section', 'seq')
- passed_value_grad: bfloat16 [4, 2048, 512], P('section', 'seq')
Inputs may be any that keep to these rules, and one draw needn't show every extreme that they name: `random_blocks`: over the 12 random blocks named by one shard's query blocks, the blocks of any one shard are named at most 2 times, and on every shard some shard's blocks exactly 2 times; within one random slot (one column) at most 1 times, and exactly 1 times for some shard. `global_blocks`: the 2 global blocks of a section are distinct. `pad_lengths`: every section has a shard with exactly 63 padding tokens.
All inputs are finite; a program needn't handle non-finite values.
Results may differ from a plain program's by a relative error of at most 0.007.
Values may be sent and summed in bfloat16 or wider, within the bound.
No kernel may reach another device: no remote copies, remote signals or barrier semaphores. Data moves between devices by JAX's collectives and lax.ppermute only.
A program may use at most 128 MiB of HBM per device.

v0:
```python
import math
import jax
import jax.numpy as jnp
from jax import lax
from jax.sharding import PartitionSpec as P

HDIM = 128
BLK = 64
GLOB = 2
RAND = 3


def extended_2(array, sides, width):
    for axis, dim in sides:
        devices, length = (lax.axis_size(axis), array.shape[dim])
        up = [(i, (i + 1) % devices) for i in range(devices - 1)]
        down = [(j, i) for i, j in up]
        last = lax.slice_in_dim(array, length - width, length, axis=dim)
        leading = lax.slice_in_dim(array, 0, width, axis=dim)
        before = lax.ppermute(last, axis, up)
        after = lax.ppermute(leading, axis, down)
        array = jnp.concatenate([before, array, after], axis=dim)
    return array


def broadcast(array, axis, root):
    mine = lax.axis_index(axis) == root
    return lax.psum(jnp.where(mine, array, jnp.zeros_like(array)), axis)


def from_behind(block, axis, distance):
    devices = range(lax.axis_size(axis))
    route = [((i - distance) % len(devices), i) for i in devices]
    return lax.ppermute(block, axis, route)


def block_backward(query_rows, grad_rows, key_tiles, value_tiles, key_live):
    nblocks, block_len, qwidth = query_rows.shape
    ntiles = key_tiles.shape[1]
    kwidth = key_tiles.shape[-1]
    heads_kv = kwidth // HDIM
    group = qwidth // kwidth
    score_scale = 1.0 / math.sqrt(HDIM)
    query_heads = jnp.moveaxis(query_rows.reshape(nblocks, block_len, heads_kv, group, HDIM), 2, 0)
    grad_heads = jnp.moveaxis(grad_rows.reshape(nblocks, block_len, heads_kv, group, HDIM), 2, 0)
    key_heads = jnp.moveaxis(key_tiles.reshape(nblocks, ntiles, block_len, heads_kv, HDIM), 3, 0)
    value_heads = jnp.moveaxis(
        value_tiles.reshape(nblocks, ntiles, block_len, heads_kv, HDIM), 3, 0
    )
    live_mask = key_live[:, None, None, :, :]

    def one_head(inputs):
        query_one, grad_one, key_one, value_one = inputs
        scores = (
            jnp.einsum("bqgd,btkd->bgqtk", query_one, key_one, preferred_element_type=jnp.float32)
            * score_scale
        )
        scores = jnp.where(live_mask, scores, -1e30)
        row_max = jnp.max(scores, axis=(3, 4), keepdims=True)
        log_total = row_max + jnp.log(
            jnp.sum(jnp.exp(scores - row_max), axis=(3, 4), keepdims=True)
        )
        probs = jnp.exp(scores - log_total)
        probs_low = probs.astype(jnp.bfloat16)
        output = jnp.einsum(
            "bgqtk,btkd->bqgd", probs_low, value_one, preferred_element_type=jnp.float32
        )
        row_dot = jnp.sum(grad_one * output, axis=-1)
        prob_grad = jnp.einsum(
            "bqgd,btkd->bgqtk", grad_one, value_one, preferred_element_type=jnp.float32
        )
        score_grad = (
            probs * (prob_grad - jnp.transpose(row_dot, (0, 2, 1))[:, :, :, None, None])
        ).astype(jnp.bfloat16)
        query_grad = (
            jnp.einsum("bgqtk,btkd->bqgd", score_grad, key_one, preferred_element_type=jnp.float32)
            * score_scale
        )
        key_grad = (
            jnp.einsum(
                "bgqtk,bqgd->btkd", score_grad, query_one, preferred_element_type=jnp.float32
            )
            * score_scale
        )
        value_grad = jnp.einsum(
            "bgqtk,bqgd->btkd", probs_low, grad_one, preferred_element_type=jnp.float32
        )
        return (query_grad, key_grad, value_grad)

    query_grad, key_grad, value_grad = lax.map(
        one_head, (query_heads, grad_heads, key_heads, value_heads)
    )
    return (
        jnp.moveaxis(query_grad, 0, 2).reshape(nblocks, block_len, qwidth),
        jnp.moveaxis(key_grad, 0, 3).reshape(nblocks, ntiles, block_len, kwidth),
        jnp.moveaxis(value_grad, 0, 3).reshape(nblocks, ntiles, block_len, kwidth),
    )


def request_plan(request_lists, this_shard, query_blocks):
    shards, count = request_lists.shape
    capacity = -(-count // shards)
    owner_ids = request_lists // query_blocks
    local_ids = request_lists % query_blocks
    order = jnp.arange(count, dtype=jnp.int32)
    earlier = order[None, :] < order[:, None]
    same_owner = owner_ids[:, :, None] == owner_ids[:, None, :]
    slot_rank = jnp.sum(same_owner & earlier[None], axis=2)
    slot_ids = jnp.arange(capacity, dtype=jnp.int32)
    chosen = (owner_ids[:, None, :] == this_shard) & (
        slot_rank[:, None, :] == slot_ids[None, :, None]
    )
    serve_block = jnp.sum(jnp.where(chosen, local_ids[:, None, :], 0), axis=2)
    slot_used = jnp.any(chosen, axis=2)
    owner_mine = lax.dynamic_index_in_dim(owner_ids, this_shard, 0, keepdims=False)
    rank_mine = lax.dynamic_index_in_dim(slot_rank, this_shard, 0, keepdims=False)
    return (serve_block, slot_used, owner_mine, rank_mine)


def serve_tiles(own_blocks, request_info):
    serve_block, slot_used = (request_info[0], request_info[1])
    shards, capacity = serve_block.shape
    gathered = jnp.take(own_blocks, serve_block.reshape(-1), axis=1)
    gathered = gathered.reshape(2, shards, capacity, own_blocks.shape[2], own_blocks.shape[3])
    return jnp.where(slot_used[None, :, :, None, None], gathered, jnp.zeros((), own_blocks.dtype))


def pick_tiles(received, request_info):
    return received[:, request_info[2], request_info[3]]


def place_terms(terms, request_info):
    serve_block = request_info[0]
    shards, capacity = serve_block.shape
    holder = jnp.zeros((2, shards, capacity, terms.shape[2], terms.shape[3]), terms.dtype)
    return holder.at[:, request_info[2], request_info[3]].set(terms)


def absorb_terms(received, request_info, query_blocks):
    serve_block, slot_used = (request_info[0], request_info[1])
    onehot = (
        slot_used[:, :, None]
        & (serve_block[:, :, None] == jnp.arange(query_blocks, dtype=jnp.int32)[None, None, :])
    ).astype(jnp.bfloat16)
    return jnp.einsum("ncq,xncsk->xqsk", onehot, received, preferred_element_type=jnp.float32)


def token_live(tile_ids, pad_sizes, query_blocks, shard_tokens, total_blocks):
    valid = (tile_ids >= 0) & (tile_ids < total_blocks)
    safe_ids = jnp.clip(tile_ids, 0, total_blocks - 1)
    owner_shard = safe_ids // query_blocks
    shards = pad_sizes.shape[0]
    pad_of = jnp.sum(
        jnp.where(owner_shard[..., None] == jnp.arange(shards, dtype=jnp.int32), pad_sizes, 0),
        axis=-1,
    )
    within = (safe_ids % query_blocks)[..., None] * BLK + jnp.arange(BLK, dtype=jnp.int32)
    return valid[..., None] & (within < (shard_tokens - pad_of)[..., None])


def body(queries, keys, values, out_grads, random_blocks, global_blocks, pad_lengths):
    query_rows = queries[0]
    key_rows = keys[0]
    value_rows = values[0]
    grad_rows = out_grads[0]
    random_table = random_blocks[0]
    global_ids = global_blocks[0]
    pad_sizes = pad_lengths[0]
    shards = lax.axis_size("seq")
    this_shard = lax.axis_index("seq")
    shard_tokens, qwidth = query_rows.shape
    kwidth = key_rows.shape[1]
    query_blocks = shard_tokens // BLK
    total_blocks = query_blocks * shards
    near = 3 + GLOB
    kvpair = jnp.stack([key_rows, value_rows])
    extended = extended_2(kvpair, (("seq", 1),), BLK)
    ext_blocks = extended.reshape(2, query_blocks + 2, BLK, kwidth)
    window = jnp.stack(
        [ext_blocks[:, offset : offset + query_blocks] for offset in range(3)], axis=2
    )
    own_blocks = kvpair.reshape(2, query_blocks, BLK, kwidth)
    global_list = []
    for glob_num in range(GLOB):
        owner_dev = global_ids[glob_num] // query_blocks
        local_tile = lax.dynamic_index_in_dim(
            own_blocks, global_ids[glob_num] % query_blocks, 1, keepdims=False
        )
        global_list.append(broadcast(local_tile, "seq", owner_dev))
    global_tiles = jnp.stack(global_list, axis=1)
    random_three = random_table.reshape(shards, query_blocks, RAND)
    slot_plans = []
    pieces = []
    for slot_num in range(RAND):
        slot_plan = request_plan(random_three[:, :, slot_num], this_shard, query_blocks)
        received = lax.all_to_all(
            serve_tiles(own_blocks, slot_plan), "seq", split_axis=1, concat_axis=1, tiled=True
        )
        pieces.append(pick_tiles(received, slot_plan))
        slot_plans.append(slot_plan)
    fetched = jnp.stack(pieces, axis=2)
    spread_global = jnp.broadcast_to(global_tiles[:, None], (2, query_blocks, GLOB, BLK, kwidth))
    all_tiles = jnp.concatenate([window, spread_global, fetched], axis=2)
    base_ids = this_shard * query_blocks + jnp.arange(query_blocks, dtype=jnp.int32)
    window_ids = base_ids[:, None] + jnp.arange(-1, 2, dtype=jnp.int32)[None, :]
    my_random = lax.dynamic_index_in_dim(random_three, this_shard, 0, keepdims=False)
    tile_ids = jnp.concatenate(
        [window_ids, jnp.broadcast_to(global_ids[None, :], (query_blocks, GLOB)), my_random], axis=1
    )
    key_live = token_live(tile_ids, pad_sizes, query_blocks, shard_tokens, total_blocks)
    query_grad, key_terms, value_terms = block_backward(
        query_rows.reshape(query_blocks, BLK, qwidth),
        grad_rows.reshape(query_blocks, BLK, qwidth),
        all_tiles[0],
        all_tiles[1],
        key_live,
    )
    contrib = jnp.stack([key_terms, value_terms])
    local_sum = contrib[:, :, 1]
    local_sum = local_sum + jnp.pad(contrib[:, 1:, 0], ((0, 0), (0, 1), (0, 0), (0, 0)))
    local_sum = local_sum + jnp.pad(contrib[:, :-1, 2], ((0, 0), (1, 0), (0, 0), (0, 0)))
    edge_out = jnp.concatenate([contrib[:, 0, 0], contrib[:, query_blocks - 1, 2]], axis=1)
    edge_in = extended_2(edge_out.astype(jnp.bfloat16), (("seq", 1),), BLK).astype(edge_out.dtype)
    local_sum = local_sum.at[:, 0].add(edge_in[:, :BLK])
    local_sum = local_sum.at[:, query_blocks - 1].add(edge_in[:, 3 * BLK :])
    global_part = jnp.sum(contrib[:, :, 3:near], axis=1)
    global_total = lax.psum(global_part, "seq")
    global_pick = (
        (global_ids[:, None] // query_blocks == this_shard)
        & (global_ids[:, None] % query_blocks == jnp.arange(query_blocks, dtype=jnp.int32)[None, :])
    ).astype(jnp.float32)
    local_sum = local_sum + jnp.einsum(
        "gq,xgsk->xqsk", global_pick, global_total, precision=lax.Precision.HIGHEST
    )
    random_terms = contrib[:, :, near:].astype(jnp.bfloat16)
    for slot_num in range(RAND):
        returned = lax.all_to_all(
            place_terms(random_terms[:, :, slot_num], slot_plans[slot_num]),
            "seq",
            split_axis=1,
            concat_axis=1,
            tiled=True,
        )
        local_sum = local_sum + absorb_terms(returned, slot_plans[slot_num], query_blocks)
    key_grad = local_sum[0].reshape(shard_tokens, kwidth).astype(jnp.bfloat16)
    value_grad = local_sum[1].reshape(shard_tokens, kwidth).astype(jnp.bfloat16)
    query_low = query_grad.reshape(shard_tokens, qwidth).astype(jnp.bfloat16)
    packed = jnp.concatenate([query_low, key_grad, value_grad], axis=-1)
    handed = from_behind(packed, "section", -1)
    return (
        handed[None, :, :qwidth],
        handed[None, :, qwidth : qwidth + kwidth],
        handed[None, :, qwidth + kwidth :],
    )


def solution(mesh):
    in_specs = (
        P("section", "seq", None),
        P("section", "seq", None),
        P("section", "seq", None),
        P("section", "seq", None),
        P("section", None, None),
        P("section", None),
        P("section", None),
    )
    out_specs = (P("section", "seq", None), P("section", "seq", None), P("section", "seq", None))
    return jax.shard_map(body, mesh=mesh, in_specs=in_specs, out_specs=out_specs, check_vma=False)
```

profile of v0, /device:TPU:1, one launch (start us, length us, event | category | flops | bytes accessed | tf_op | source)
XLA Modules:
  0.0 463.5 jit_solution(16679181156214838141)
XLA Ops:
  17.7 6.4 %all-to-all-start = ((bf16[2,8,1,64,512]{4,3,0,2,1:T(8,128)(2,1)}), bf16[2,8,1,64,512]{4,3,0,2,1:T(8,128)(2,1)S(1)}, u32[]{:S(2)}, u32[]{:S(2)}) async-start(bf16[2,8,1,64,512]{4,3,0,2,1:T(8,128)(2,1)} %fusion.54), calls=%async_computation | async-start | bytes 2097152 | tf_op jit(solution)/shard_map/all_to_all | solution.py:196
  35.6 15.4 %all-to-all-done = bf16[2,8,1,64,512]{4,3,0,2,1:T(8,128)(2,1)S(1)} async-done(((bf16[2,8,1,64,512]{4,3,0,2,1:T(8,128)(2,1)}), bf16[2,8,1,64,512]{4,3,0,2,1:T(8,128)(2,1)S(1)}, u32[]{:S(2)}, u32[]{:S(2)}) %all-to-all-start) | async-done | bytes 1048608 | tf_op jit(solution)/shard_map/all_to_all | solution.py:196
  51.1 5.3 %all-to-all-start.1 = ((bf16[2,8,1,64,512]{4,3,0,2,1:T(8,128)(2,1)}), bf16[2,8,1,64,512]{4,3,0,2,1:T(8,128)(2,1)S(1)}, u32[]{:S(2)}, u32[]{:S(2)}) async-start(bf16[2,8,1,64,512]{4,3,0,2,1:T(8,128)(2,1)} %fusion.53), calls=%async_computation.1 | async-start | bytes 2097152 | tf_op jit(solution)/shard_map/all_to_all | solution.py:196
  60.3 21.6 %all-to-all-done.1 = bf16[2,8,1,64,512]{4,3,0,2,1:T(8,128)(2,1)S(1)} async-done(((bf16[2,8,1,64,512]{4,3,0,2,1:T(8,128)(2,1)}), bf16[2,8,1,64,512]{4,3,0,2,1:T(8,128)(2,1)S(1)}, u32[]{:S(2)}, u32[]{:S(2)}) %all-to-all-start.1) | async-done | bytes 1048608 | tf_op jit(solution)/shard_map/all_to_all | solution.py:196
  82.0 4.8 %all-to-all-start.2 = ((bf16[2,8,1,64,512]{4,3,0,2,1:T(8,128)(2,1)}), bf16[2,8,1,64,512]{4,3,0,2,1:T(8,128)(2,1)}, u32[]{:S(2)}, u32[]{:S(2)}) async-start(bf16[2,8,1,64,512]{4,3,0,2,1:T(8,128)(2,1)} %fusion.52), calls=%async_computation.2 | async-start | bytes 2097152 | tf_op jit(solution)/shard_map/all_to_all | solution.py:196
  95.4 21.6 %all-reduce.8.cloned.1.call-done = (bf16[2,1,64,512]{3,2,1,0:T(8,128)(2,1)}, bf16[2,1,64,512]{3,2,1,0:T(8,128)(2,1)}) async-done(((bf16[2,1,64,512]{3,2,1,0:T(8,128)(2,1)}, bf16[2,1,64,512]{3,2,1,0:T(8,128)(2,1)}), (bf16[2,1,64,512]{3,2,1,0:T(8,128)(2,1)}, bf16[2,1,64,512]{3,2,1,0:T(8,128)(2,1)})) %all-reduce.8.cloned.1.call-update) | async-done | bytes 262160 | tf_op jit(solution)/shard_map/psum | solution.py:28
  127.2 4.0 fusion.130
  135.4 4.0 reshape_squeeze.13
  142.8 77.5 %while.17 = (s32[]{:T(128)}, bf16[4,4,64,8,128]{4,2,3,1,0:T(8,128)(2,1)}, f32[4,4,8,64,128]{4,3,2,1,0:T(8,128)}, f32[4,4,8,64,128]{4,3,2,1,0:T(8,128)}, bf16[4,4...) while((s32[]{:T(128)}, ...), condition=%wide.region_16.18_spmd.clone, body=%wide.region_12.17_spmd.clone.sunk | while | flops 1633945600 | bytes 56234432 | solution.py:90
  220.3 7.8 %copy.163 = f32[4,8,64,4,128]{4,3,2,0,1:T(4,128)} copy(f32[4,8,64,4,128]{4,2,1,0,3:T(8,128)} %bitcast.563) | data formatting | bytes 8388608 | tf_op jit(solution)/shard_map/transpose | solution.py:95
  228.1 5.5 %stack_reshape.6 = f32[1,4,8,64,512]{4,3,0,1,2:T(8,128)} reshape(f32[4,8,64,4,128]{4,3,2,0,1:T(4,128)} %copy.163) | data formatting | bytes 8388608 | tf_op jit(solution)/shard_map/stack;reshape | solution.py:218
  233.6 5.0 %constant_dynamic-update-slice_fusion.3 = f32[2,4,8,64,512]{4,3,0,1,2:T(8,128)} fusion(f32[1,4,8,64,512]{4,3,0,1,2:T(8,128)} %stack_reshape.6), kind=kLoop, calls=%fused_computation.124 | loop fusion | bytes 8388608
  238.6 5.6 %copy.164 = f32[4,8,64,4,128]{4,3,2,0,1:T(4,128)} copy(f32[4,8,64,4,128]{4,2,1,0,3:T(8,128)S(1)} %bitcast.564) | data formatting | bytes 8388608 | tf_op jit(solution)/shard_map/transpose | solution.py:96
  244.1 5.5 %stack_reshape.7 = f32[1,4,8,64,512]{4,3,0,1,2:T(8,128)} reshape(f32[4,8,64,4,128]{4,3,2,0,1:T(4,128)} %copy.164) | data formatting | bytes 8388608 | tf_op jit(solution)/shard_map/stack;reshape | solution.py:218
  249.6 4.8 %constant_dynamic-update-slice_fusion.2 = f32[2,4,8,64,512]{4,3,0,1,2:T(8,128)} fusion(f32[2,4,8,64,512]{4,3,0,1,2:T(8,128)} %constant_dynamic-update-slice_fusion.3, f32[1,4,8,64,512]{4,3,0,1,2:T(8,128)} %stack_reshape.7), kind=kLoop, calls=%fused_computation.123 | loop fusion | bytes 8388608 | tf_op jit(solution)/shard_map/stack | solution.py:218
  254.4 4.0 convert.13
  268.6 22.3 %all-to-all-done.3 = bf16[2,8,1,64,512]{4,3,0,2,1:T(8,128)(2,1)S(1)} async-done(((bf16[2,8,1,64,512]{4,3,0,2,1:T(8,128)(2,1)}), bf16[2,8,1,64,512]{4,3,0,2,1:T(8,128)(2,1)S(1)}, u32[]{:S(2)}, u32[]{:S(2)}) %all-to-all-start.3) | async-done | bytes 1048608 | tf_op jit(solution)/shard_map/all_to_all | solution.py:237
  290.9 5.1 %all-to-all-start.4 = ((bf16[2,8,1,64,512]{4,3,0,2,1:T(8,128)(2,1)}), bf16[2,8,1,64,512]{4,3,0,2,1:T(8,128)(2,1)}, u32[]{:S(2)}, u32[]{:S(2)}) async-start(bf16[2,8,1,64,512]{4,3,0,2,1:T(8,128)(2,1)} %copy.173), calls=%async_computation.4 | async-start | bytes 2097152 | tf_op jit(solution)/shard_map/all_to_all | solution.py:237
  301.3 19.4 %all-to-all-done.4 = bf16[2,8,1,64,512]{4,3,0,2,1:T(8,128)(2,1)} async-done(((bf16[2,8,1,64,512]{4,3,0,2,1:T(8,128)(2,1)}), bf16[2,8,1,64,512]{4,3,0,2,1:T(8,128)(2,1)}, u32[]{:S(2)}, u32[]{:S(2)}) %all-to-all-start.4) | async-done | bytes 1048608 | tf_op jit(solution)/shard_map/all_to_all | solution.py:237
  320.6 5.1 %all-to-all-start.5 = ((bf16[2,8,1,64,512]{4,3,0,2,1:T(8,128)(2,1)}), bf16[2,8,1,64,512]{4,3,0,2,1:T(8,128)(2,1)}, u32[]{:S(2)}, u32[]{:S(2)}) async-start(bf16[2,8,1,64,512]{4,3,0,2,1:T(8,128)(2,1)} %copy.176), calls=%async_computation.5 | async-start | bytes 2097152 | tf_op jit(solution)/shard_map/all_to_all | solution.py:237
  336.6 4.3 copy.162
  350.6 6.1 %scatter-add.9 = f32[2,4,64,512]{3,1,2,0:T(4,128)} dynamic-update-slice(f32[2,4,64,512]{3,1,2,0:T(4,128)} %copy.167, f32[2,1,64,512]{3,1,2,0:T(1,128)S(1)} %copy_add_fusion, s32[]{:T(128)} %constant.241.clone.1, s32[]{:T(128)} %constant.245.clone.1, s32[]{:T(128)} %constant.241.clone.1, s32[]{:T(128)} %constant.241.clone.1) | dynamic-update-slice | bytes 524292 | tf_op jit(solution)/shard_map/scatter-add | solution.py:225
  356.8 54.0 %all-reduce.6.cloned.1.call-done = f32[2,2,64,512]{3,1,2,0:T(2,128)} async-done(((f32[2,2,64,512]{3,1,2,0:T(2,128)}), f32[2,2,64,512]{3,1,2,0:T(2,128)}) %all-reduce.6.cloned.1.call-update) | async-done | bytes 524304 | tf_op jit(solution)/shard_map/psum | solution.py:227
  424.0 30.4 %collective-permute-done.4 = bf16[256,5120]{1,0:T(8,128)(2,1)S(1)} collective-permute-done((bf16[256,5120]{1,0:T(8,128)(2,1)S(1)}, bf16[256,5120]{1,0:T(8,128)(2,1)S(1)}, u32[]{:S(2)}, u32[]{:S(2)}) %collective-permute-start.4) | collective-permute-done | bytes 2621472 | tf_op jit(solution)/shard_map/ppermute | solution.py:34
  (222 shorter events, 175.5 us)
Async XLA Ops:
  9.2 83.6 %collective-permute-start = (bf16[2,64,512]{2,1,0:T(8,128)(2,1)S(1)}, bf16[2,64,512]{2,1,0:T(8,128)(2,1)S(1)}, u32[]{:S(2)}, u32[]{:S(2)}) collective-permute-start(bf16[2,64,512]{2,1,0:T(8,128)(2,1)S(1)} %get-tuple-element.194), channel_id=1, source_target_pairs={{0,1},{1,2},{2,3},{3,4},{4,5},{5,6},{6,7},{8,9},{9,10},{10,11},{11... | collective-permute-start | bytes 393224 | tf_op jit(solution)/shard_map/ppermute | solution.py:20
  13.1 79.7 %collective-permute-start.1 = (bf16[2,64,512]{2,1,0:T(8,128)(2,1)S(1)}, bf16[2,64,512]{2,1,0:T(8,128)(2,1)S(1)}, u32[]{:S(2)}, u32[]{:S(2)}) collective-permute-start(bf16[2,64,512]{2,1,0:T(8,128)(2,1)S(1)} %get-tuple-element.195), channel_id=1, source_target_pairs={{1,0},{2,1},{3,2},{4,3},{5,4},{6,5},{7,6},{9,8},{10,9},{11,10},{12... | collective-permute-start | bytes 393224 | tf_op jit(solution)/shard_map/ppermute | solution.py:21
  17.7 33.3 %all-to-all-start = ((bf16[2,8,1,64,512]{4,3,0,2,1:T(8,128)(2,1)}), bf16[2,8,1,64,512]{4,3,0,2,1:T(8,128)(2,1)S(1)}, u32[]{:S(2)}, u32[]{:S(2)}) async-start(bf16[2,8,1,64,512]{4,3,0,2,1:T(8,128)(2,1)} %fusion.54), calls=%async_computation | async-start | bytes 2097152 | tf_op jit(solution)/shard_map/all_to_all | solution.py:196
  24.1 92.9 %all-reduce.8.cloned.1.call-start = ((), (), s32[]{:S(2)}) async-start(), calls=%async_computation.7 | async-start | bytes 524288 | tf_op jit(solution)/shard_map/psum | solution.py:28
  31.8 24.8 %copy-start.22 = (s32[1,8]{1,0:T(1,128)S(1)}, s32[1,8]{1,0:T(1,128)}, u32[]{:S(2)}) copy-start(s32[1,8]{1,0:T(1,128)} %param.21) | copy-start | bytes 100
  32.6 27.7 %copy-start.9 = (pred[8]{0:T(512)(128)(4,1)}, pred[8]{0:T(512)(128)(4,1)S(1)}, u32[]{:S(2)}) copy-start(pred[8]{0:T(512)(128)(4,1)S(1)} %get-tuple-element.169) | copy-start | bytes 28
  32.7 27.7 %copy-start.15 = (s32[8]{0:T(128)}, s32[8]{0:T(128)S(1)}, u32[]{:S(2)}) copy-start(s32[8]{0:T(128)S(1)} %fusion.87) | copy-start | bytes 100
  51.1 30.9 %all-to-all-start.1 = ((bf16[2,8,1,64,512]{4,3,0,2,1:T(8,128)(2,1)}), bf16[2,8,1,64,512]{4,3,0,2,1:T(8,128)(2,1)S(1)}, u32[]{:S(2)}, u32[]{:S(2)}) async-start(bf16[2,8,1,64,512]{4,3,0,2,1:T(8,128)(2,1)} %fusion.53), calls=%async_computation.1 | async-start | bytes 2097152 | tf_op jit(solution)/shard_map/all_to_all | solution.py:196
  82.0 42.5 %all-to-all-start.2 = ((bf16[2,8,1,64,512]{4,3,0,2,1:T(8,128)(2,1)}), bf16[2,8,1,64,512]{4,3,0,2,1:T(8,128)(2,1)}, u32[]{:S(2)}, u32[]{:S(2)}) async-start(bf16[2,8,1,64,512]{4,3,0,2,1:T(8,128)(2,1)} %fusion.52), calls=%async_computation.2 | async-start | bytes 2097152 | tf_op jit(solution)/shard_map/all_to_all | solution.py:196
  262.9 33.1 %copy-start.21 = (s32[1,2]{1,0:T(1,128)S(1)}, s32[1,2]{1,0:T(1,128)}, u32[]{:S(2)}) copy-start(s32[1,2]{1,0:T(1,128)} %param.20) | copy-start | bytes 28
  262.9 28.0 %all-to-all-start.3 = ((bf16[2,8,1,64,512]{4,3,0,2,1:T(8,128)(2,1)}), bf16[2,8,1,64,512]{4,3,0,2,1:T(8,128)(2,1)S(1)}, u32[]{:S(2)}, u32[]{:S(2)}) async-start(bf16[2,8,1,64,512]{4,3,0,2,1:T(8,128)(2,1)} %copy.170), calls=%async_computation.3 | async-start | bytes 2097152 | tf_op jit(solution)/shard_map/all_to_all | solution.py:237
  266.6 29.6 %copy-start.17 = (s32[4]{0:T(128)S(1)}, s32[4]{0:T(128)}, u32[]{:S(2)}) copy-start(s32[4]{0:T(128)} %get-tuple-element.204) | copy-start | bytes 52
  290.9 29.7 %all-to-all-start.4 = ((bf16[2,8,1,64,512]{4,3,0,2,1:T(8,128)(2,1)}), bf16[2,8,1,64,512]{4,3,0,2,1:T(8,128)(2,1)}, u32[]{:S(2)}, u32[]{:S(2)}) async-start(bf16[2,8,1,64,512]{4,3,0,2,1:T(8,128)(2,1)} %copy.173), calls=%async_computation.4 | async-start | bytes 2097152 | tf_op jit(solution)/shard_map/all_to_all | solution.py:237
  320.6 97.9 %all-to-all-start.5 = ((bf16[2,8,1,64,512]{4,3,0,2,1:T(8,128)(2,1)}), bf16[2,8,1,64,512]{4,3,0,2,1:T(8,128)(2,1)}, u32[]{:S(2)}, u32[]{:S(2)}) async-start(bf16[2,8,1,64,512]{4,3,0,2,1:T(8,128)(2,1)} %copy.176), calls=%async_computation.5 | async-start | bytes 2097152 | tf_op jit(solution)/shard_map/all_to_all | solution.py:237
  325.7 85.0 %all-reduce.6.cloned.1.call-start = ((), (), s32[]{:S(2)}) async-start(), calls=%async_computation.6 | async-start | bytes 1048576 | tf_op jit(solution)/shard_map/psum | solution.py:227
  327.9 15.9 %collective-permute-start.2 = (bf16[2,64,512]{2,1,0:T(8,128)(2,1)S(1)}, bf16[2,64,512]{2,1,0:T(8,128)(2,1)}, u32[]{:S(2)}, u32[]{:S(2)}) collective-permute-start(bf16[2,64,512]{2,1,0:T(8,128)(2,1)S(1)} %get-tuple-element.184), channel_id=1, source_target_pairs={{0,1},{1,2},{2,3},{3,4},{4,5},{5,6},{6,7},{8,9},{9,10},{10,11},{11... | collective-permute-start | bytes 393224 | tf_op jit(solution)/shard_map/ppermute | solution.py:20
  331.6 12.2 %collective-permute-start.3 = (bf16[2,64,512]{2,1,0:T(8,128)(2,1)}, bf16[2,64,512]{2,1,0:T(8,128)(2,1)}, u32[]{:S(2)}, u32[]{:S(2)}) collective-permute-start(bf16[2,64,512]{2,1,0:T(8,128)(2,1)} %get-tuple-element.185), channel_id=1, source_target_pairs={{1,0},{2,1},{3,2},{4,3},{5,4},{6,5},{7,6},{9,8},{10,9},{11,10},{12... | collective-permute-start | bytes 393224 | tf_op jit(solution)/shard_map/ppermute | solution.py:21
  343.7 69.7 %copy-start.6 = (pred[8]{0:T(512)(128)(4,1)S(1)}, pred[8]{0:T(512)(128)(4,1)}, u32[]{:S(2)}) copy-start(pred[8]{0:T(512)(128)(4,1)} %copy-done.5) | copy-start | bytes 28
  343.8 69.7 %copy-start.12 = (s32[8]{0:T(128)S(1)}, s32[8]{0:T(128)}, u32[]{:S(2)}) copy-start(s32[8]{0:T(128)} %copy-done.11) | copy-start | bytes 100
  349.3 66.1 %copy-start.8 = (pred[8]{0:T(512)(128)(4,1)S(1)}, pred[8]{0:T(512)(128)(4,1)}, u32[]{:S(2)}) copy-start(pred[8]{0:T(512)(128)(4,1)} %copy-done.7) | copy-start | bytes 28
  349.4 66.1 %copy-start.14 = (s32[8]{0:T(128)S(1)}, s32[8]{0:T(128)}, u32[]{:S(2)}) copy-start(s32[8]{0:T(128)} %copy-done.13) | copy-start | bytes 100
  356.8 61.8 %copy-start.10 = (pred[8]{0:T(512)(128)(4,1)S(1)}, pred[8]{0:T(512)(128)(4,1)}, u32[]{:S(2)}) copy-start(pred[8]{0:T(512)(128)(4,1)} %copy-done.9) | copy-start | bytes 28
  356.8 61.8 %copy-start.16 = (s32[8]{0:T(128)S(1)}, s32[8]{0:T(128)}, u32[]{:S(2)}) copy-start(s32[8]{0:T(128)} %copy-done.15) | copy-start | bytes 100
  421.4 33.0 %collective-permute-start.4 = (bf16[256,5120]{1,0:T(8,128)(2,1)S(1)}, bf16[256,5120]{1,0:T(8,128)(2,1)S(1)}, u32[]{:S(2)}, u32[]{:S(2)}) collective-permute-start(bf16[256,5120]{1,0:T(8,128)(2,1)S(1)} %pad_maximum_fusion), channel_id=1, source_target_pairs={{8,0},{16,8},{24,16},{0,24},{9,1},{17,9},{25,17},{1,25},{10,2},{18... | collective-permute-start | bytes 7864328 | tf_op jit(solution)/shard_map/ppermute | solution.py:34
  (15 other events, 131.4 us)
Sparse Core Ops, SparseCore 0:
  30.9 86.1 all-reduce.7
  334.3 76.4 all-reduce.5
where the time goes:
time: 465 us; the launch traced here: 463 us
  waiting for transfers between devices  185 us (40%)
  local copies, waits for them, and re-layouts  112 us (24%)
  matrix products  73.1 us (16%)
  starting transfers between devices  43.5 us (9%)
  other arithmetic  30.4 us (7%)
  between operations  19.9 us (4%)
    psum x1, waiting for transfers between devices, body(): global_total = lax.psum(global_part, 'seq')  54 us
    all_to_all x3, waiting for transfers between devices, body(): lax.all_to_all(place_terms(random_terms[:, :, slot_num], slot_plans[slot_...  41.7 us
    all_to_all x3, waiting for transfers between devices, body(): lax.all_to_all(serve_tiles(own_blocks, slot_plan), 'seq', split_axis=1, c...  37.1 us
    ppermute x1, waiting for transfers between devices, from_behind(): return lax.ppermute(block, axis, route)  30.4 us
    unnamed x56, local copies, waits for them, and re-layouts  24.8 us
    psum x1, waiting for transfers between devices, broadcast(): return lax.psum(jnp.where(mine, array, jnp.zeros_like(array)), axis)  21.6 us
    all_to_all x3, starting transfers between devices, body(): lax.all_to_all(serve_tiles(own_blocks, slot_plan), 'seq', split_axis=1, c...  16.5 us
    another operation x3, local copies, waits for them, and re-layouts, body(): contrib = jnp.stack([key_terms, value_terms])  15.8 us
  transfers between devices with their start and end apart: 13, of which 7 were waited for; matrix products, arithmetic and copies ran while one was open for 15% of the time, Pallas kernels for 0%

commit v1 on v0

--- a/solution.py
+++ b/solution.py
@@ -8,6 +8,29 @@
 BLK = 64
 GLOB = 2
 RAND = 3
+
+
+def split_up(x, dim, peers):
+    shape = x.shape
+    tiles = x.reshape(*shape[:dim], peers, shape[dim] // peers, *shape[dim + 1 :])
+    return jnp.moveaxis(tiles, dim, 0)
+
+
+def in_order(blocks, dim):
+    blocks = jnp.moveaxis(blocks, 0, dim)
+    lengths = blocks.shape
+    return blocks.reshape(*lengths[:dim], lengths[dim] * lengths[dim + 1], *lengths[dim + 2 :])
+
+
+def exchange_in_pairs(x, axis, split_dim, concat_dim):
+    peers, mine = (lax.axis_size(axis), lax.axis_index(axis))
+    tiles = split_up(x, split_dim, peers)
+    finished = [tiles[mine]]
+    for step in range(1, peers):
+        sent = tiles[mine ^ step]
+        finished.append(lax.ppermute(sent, axis, [(i, i ^ step) for i in range(peers)]))
+    tiles = jnp.stack(finished)[mine ^ jnp.arange(peers)]
+    return in_order(tiles, concat_dim)
 
 
 def extended_2(array, sides, width):
@@ -234,12 +257,8 @@
     )
     random_terms = contrib[:, :, near:].astype(jnp.bfloat16)
     for slot_num in range(RAND):
-        returned = lax.all_to_all(
-            place_terms(random_terms[:, :, slot_num], slot_plans[slot_num]),
-            "seq",
-            split_axis=1,
-            concat_axis=1,
-            tiled=True,
+        returned = exchange_in_pairs(
+            place_terms(random_terms[:, :, slot_num], slot_plans[slot_num]), "seq", 1, 1
         )
         local_sum = local_sum + absorb_terms(returned, slot_plans[slot_num], query_blocks)
     key_grad = local_sum[0].reshape(shard_tokens, kwidth).astype(jnp.bfloat16)

time: 465 us -> 436 us (0.938); the launches traced: 463 us -> 428 us
  waiting for transfers between devices: 185 us -> 98.4 us
  starting transfers between devices: 43.5 us -> 70.9 us
  local copies, waits for them, and re-layouts: 112 us -> 139 us
    psum x1, waiting for transfers between devices: 54 us -> 0.01 us  [body(): global_total = lax.psum(global_part, 'seq')]
    all_to_all x3 -> x0, waiting for transfers between devices: 41.7 us -> none  [body(): lax.all_to_all(place_terms(random_terms[:, :, slot_num], slot_plans[slot_...]
    ppermute x0 -> x21, starting transfers between devices: none -> 38.6 us  [exchange_in_pairs(): lax.ppermute(sent, axis, [(i, i ^ step) for i in range(peers)])]
    unnamed x56 -> x89, local copies, waits for them, and re-layouts: 24.8 us -> 47.3 us
    all_to_all x3 -> x0, starting transfers between devices: 13.9 us -> none  [body(): lax.all_to_all(place_terms(random_terms[:, :, slot_num], slot_plans[slot_...]
    ppermute x0 -> x21, waiting for transfers between devices: none -> 9.12 us  [exchange_in_pairs(): lax.ppermute(sent, axis, [(i, i ^ step) for i in range(peers)])]
    gather x0 -> x3, local copies, waits for them, and re-layouts: none -> 7.89 us  [exchange_in_pairs(): tiles = jnp.stack(finished)[mine ^ jnp.arange(peers)]]
    all_to_all x3, waiting for transfers between devices: 37.1 us -> 32.4 us  [body(): lax.all_to_all(serve_tiles(own_blocks, slot_plan), 'seq', split_axis=1, c...]
  transfers between devices with their start and end apart: 13 -> 31, of which waited for: 7 -> 7; matrix products, arithmetic and copies ran while one was open for 15% -> 19% of each run, Pallas kernels for 0% -> 0%
where the time goes in v1:
time: 436 us; the launch traced here: 428 us
  local copies, waits for them, and re-layouts  139 us (32%)
  waiting for transfers between devices  98.4 us (23%)
  starting transfers between devices  70.9 us (16%)
  matrix products  69.4 us (16%)
  other arithmetic  29.6 us (7%)
  between operations  20.3 us (5%)
    unnamed x89, local copies, waits for them, and re-layouts  47.3 us
    ppermute x21, starting transfers between devices, exchange_in_pairs(): lax.ppermute(sent, axis, [(i, i ^ step) for i in range(peers)])  38.6 us
    all_to_all x3, waiting for transfers between devices, body(): lax.all_to_all(serve_tiles(own_blocks, slot_plan), 'seq', split_axis=1, c...  32.4 us
    ppermute x1, waiting for transfers between devices, from_behind(): return lax.ppermute(block, axis, route)  30.6 us
    psum x1, waiting for transfers between devices, broadcast(): return lax.psum(jnp.where(mine, array, jnp.zeros_like(array)), axis)  26.2 us
    all_to_all x3, starting transfers between devices, body(): lax.all_to_all(serve_tiles(own_blocks, slot_plan), 'seq', split_axis=1, c...  16.5 us
    another operation x3, local copies, waits for them, and re-layouts, body(): contrib = jnp.stack([key_terms, value_terms])  15.8 us
    dot_general x4, matrix products, one_head(): jnp.einsum('bgqtk,bqgd->btkd', probs_low, grad_one, preferred_element_typ...  14.3 us
  transfers between devices with their start and end apart: 31, of which 7 were waited for; matrix products, arithmetic and copies ran while one was open for 19% of the time, Pallas kernels for 0%

profile of v1, /device:TPU:1, one launch (start us, length us, event | category | flops | bytes accessed | tf_op | source)
XLA Modules:
  0.0 428.1 jit_solution(7219543732797317226)
XLA Ops:
  17.7 6.4 %all-to-all-start = ((bf16[2,8,1,64,512]{4,3,0,2,1:T(8,128)(2,1)}), bf16[2,8,1,64,512]{4,3,0,2,1:T(8,128)(2,1)}, u32[]{:S(2)}, u32[]{:S(2)}) async-start(bf16[2,8,1,64,512]{4,3,0,2,1:T(8,128)(2,1)} %fusion.51), calls=%async_computation | async-start | bytes 2097152 | tf_op jit(solution)/shard_map/all_to_all | solution.py:219
  34.9 16.3 %all-to-all-done = bf16[2,8,1,64,512]{4,3,0,2,1:T(8,128)(2,1)} async-done(((bf16[2,8,1,64,512]{4,3,0,2,1:T(8,128)(2,1)}), bf16[2,8,1,64,512]{4,3,0,2,1:T(8,128)(2,1)}, u32[]{:S(2)}, u32[]{:S(2)}) %all-to-all-start) | async-done | bytes 1048608 | tf_op jit(solution)/shard_map/all_to_all | solution.py:219
  51.2 5.3 %all-to-all-start.1 = ((bf16[2,8,1,64,512]{4,3,0,2,1:T(8,128)(2,1)}), bf16[2,8,1,64,512]{4,3,0,2,1:T(8,128)(2,1)S(1)}, u32[]{:S(2)}, u32[]{:S(2)}) async-start(bf16[2,8,1,64,512]{4,3,0,2,1:T(8,128)(2,1)} %fusion.50), calls=%async_computation.1 | async-start | bytes 2097152 | tf_op jit(solution)/shard_map/all_to_all | solution.py:219
  65.9 16.1 %all-to-all-done.1 = bf16[2,8,1,64,512]{4,3,0,2,1:T(8,128)(2,1)S(1)} async-done(((bf16[2,8,1,64,512]{4,3,0,2,1:T(8,128)(2,1)}), bf16[2,8,1,64,512]{4,3,0,2,1:T(8,128)(2,1)S(1)}, u32[]{:S(2)}, u32[]{:S(2)}) %all-to-all-start.1) | async-done | bytes 1048608 | tf_op jit(solution)/shard_map/all_to_all | solution.py:219
  82.1 4.8 %all-to-all-start.2 = ((bf16[2,8,1,64,512]{4,3,0,2,1:T(8,128)(2,1)}), bf16[2,8,1,64,512]{4,3,0,2,1:T(8,128)(2,1)S(1)}, u32[]{:S(2)}, u32[]{:S(2)}) async-start(bf16[2,8,1,64,512]{4,3,0,2,1:T(8,128)(2,1)} %fusion.49), calls=%async_computation.2 | async-start | bytes 2097152 | tf_op jit(solution)/shard_map/all_to_all | solution.py:219
  90.7 26.2 %all-reduce.8.cloned.1.call-done = (bf16[2,1,64,512]{3,2,1,0:T(8,128)(2,1)}, bf16[2,1,64,512]{3,2,1,0:T(8,128)(2,1)}) async-done(((bf16[2,1,64,512]{3,2,1,0:T(8,128)(2,1)}, bf16[2,1,64,512]{3,2,1,0:T(8,128)(2,1)}), (bf16[2,1,64,512]{3,2,1,0:T(8,128)(2,1)}, bf16[2,1,64,512]{3,2,1,0:T(8,128)(2,1)})) %all-reduce.8.cloned.1.call-update) | async-done | bytes 262160 | tf_op jit(solution)/shard_map/psum | solution.py:51
  132.7 4.0 reshape_squeeze.13
  140.2 77.6 %while.17 = (s32[]{:T(128)}, bf16[4,4,64,8,128]{4,2,3,1,0:T(8,128)(2,1)}, f32[4,4,8,64,128]{4,3,2,1,0:T(8,128)}, f32[4,4,8,64,128]{4,3,2,1,0:T(8,128)}, bf16[4,4...) while((s32[]{:T(128)}, ...), condition=%wide.region_16.18_spmd.clone, body=%wide.region_12.17_spmd.clone.sunk | while | flops 1633945600 | bytes 56234432 | solution.py:113
  217.9 7.8 %copy.189 = f32[4,8,64,4,128]{4,3,2,0,1:T(4,128)} copy(f32[4,8,64,4,128]{4,2,1,0,3:T(8,128)} %bitcast.661) | data formatting | bytes 8388608 | tf_op jit(solution)/shard_map/transpose | solution.py:118
  225.7 5.5 %stack_reshape.6 = f32[1,4,8,64,512]{4,3,0,1,2:T(8,128)} reshape(f32[4,8,64,4,128]{4,3,2,0,1:T(4,128)} %copy.189) | data formatting | bytes 8388608 | tf_op jit(solution)/shard_map/stack;reshape | solution.py:241
  231.1 5.1 %constant_dynamic-update-slice_fusion.3 = f32[2,4,8,64,512]{4,3,0,1,2:T(8,128)} fusion(f32[1,4,8,64,512]{4,3,0,1,2:T(8,128)} %stack_reshape.6), kind=kLoop, calls=%fused_computation.169 | loop fusion | bytes 8388608
  236.2 5.5 %copy.190 = f32[4,8,64,4,128]{4,3,2,0,1:T(4,128)} copy(f32[4,8,64,4,128]{4,2,1,0,3:T(8,128)S(1)} %bitcast.662) | data formatting | bytes 8388608 | tf_op jit(solution)/shard_map/transpose | solution.py:119
  241.7 5.5 %stack_reshape.7 = f32[1,4,8,64,512]{4,3,0,1,2:T(8,128)} reshape(f32[4,8,64,4,128]{4,3,2,0,1:T(4,128)} %copy.190) | data formatting | bytes 8388608 | tf_op jit(solution)/shard_map/stack;reshape | solution.py:241
  247.2 4.9 %constant_dynamic-update-slice_fusion.2 = f32[2,4,8,64,512]{4,3,0,1,2:T(8,128)} fusion(f32[2,4,8,64,512]{4,3,0,1,2:T(8,128)} %constant_dynamic-update-slice_fusion.3, f32[1,4,8,64,512]{4,3,0,1,2:T(8,128)} %stack_reshape.7), kind=kLoop, calls=%fused_computation.168 | loop fusion | bytes 8388608 | tf_op jit(solution)/shard_map/stack | solution.py:241
  252.1 4.0 convert.13
  279.6 4.3 %copy.188 = bf16[4,64,4,8,128]{4,3,2,1,0:T(8,128)(2,1)} copy(bf16[4,64,4,8,128]{4,1,3,0,2:T(8,128)(2,1)} %bitcast.577) | data formatting | bytes 4194304 | tf_op jit(solution)/shard_map/convert_element_type | solution.py:266
  304.0 6.2 %collective-permute-start.12 = (bf16[2,1,1,64,512]{4,3,0,2,1:T(8,128)(2,1)}, bf16[2,1,1,64,512]{4,3,0,2,1:T(8,128)(2,1)}, u32[]{:S(2)}, u32[]{:S(2)}) collective-permute-start(bf16[2,1,1,64,512]{4,3,0,2,1:T(8,128)(2,1)} %get-tuple-element.213), channel_id=1, source_target_pairs={{0,2},{1,3},{2,0},{3,1},{4,6},{5,7},{6,4},{7,5},{8,10},{9,11},{10,... | collective-permute-start | bytes 393224 | tf_op jit(solution)/shard_map/ppermute | solution.py:31
  310.2 5.2 %collective-permute-done.22 = bf16[2,1,1,64,512]{4,3,0,2,1:T(8,128)(2,1)S(1)} collective-permute-done((bf16[2,1,1,64,512]{4,3,0,2,1:T(8,128)(2,1)S(1)}, bf16[2,1,1,64,512]{4,3,0,2,1:T(8,128)(2,1)S(1)}, u32[]{:S(2)}, u32[]{:S(2)}) %collective-permute-start.22) | collective-permute-done | bytes 131104 | tf_op jit(solution)/shard_map/ppermute | solution.py:31
  318.0 5.3 %collective-permute-start.15 = (bf16[2,1,1,64,512]{4,3,0,2,1:T(8,128)(2,1)}, bf16[2,1,1,64,512]{4,3,0,2,1:T(8,128)(2,1)}, u32[]{:S(2)}, u32[]{:S(2)}) collective-permute-start(bf16[2,1,1,64,512]{4,3,0,2,1:T(8,128)(2,1)} %get-tuple-element.210), channel_id=1, source_target_pairs={{0,5},{1,4},{2,7},{3,6},{4,1},{5,0},{6,3},{7,2},{8,13},{9,12},{10,... | collective-permute-start | bytes 393224 | tf_op jit(solution)/shard_map/ppermute | solution.py:31
  327.9 4.5 %collective-permute-start.17 = (bf16[2,1,1,64,512]{4,3,0,2,1:T(8,128)(2,1)}, bf16[2,1,1,64,512]{4,3,0,2,1:T(8,128)(2,1)S(1)}, u32[]{:S(2)}, u32[]{:S(2)}) collective-permute-start(bf16[2,1,1,64,512]{4,3,0,2,1:T(8,128)(2,1)} %get-tuple-element.208), channel_id=1, source_target_pairs={{0,7},{1,6},{2,5},{3,4},{4,3},{5,2},{6,1},{7,0},{8,15},{9,14},{10,... | collective-permute-start | bytes 393224 | tf_op jit(solution)/shard_map/ppermute | solution.py:31
  352.3 4.0 collective-permute-start.10
  369.6 6.1 %scatter-add.9 = f32[2,4,64,512]{3,1,2,0:T(4,128)} dynamic-update-slice(f32[2,4,64,512]{3,1,2,0:T(4,128)} %copy.193, f32[2,1,64,512]{3,1,2,0:T(1,128)S(1)} %copy_add_fusion, s32[]{:T(128)} %constant.250.clone.1, s32[]{:T(128)} %constant.254.clone.1, s32[]{:T(128)} %constant.250.clone.1, s32[]{:T(128)} %constant.250.clone.1) | dynamic-update-slice | bytes 524292 | tf_op jit(solution)/shard_map/scatter-add | solution.py:248
  382.8 5.3 %collective-permute-start.25 = (bf16[256,5120]{1,0:T(8,128)(2,1)S(1)}, bf16[256,5120]{1,0:T(8,128)(2,1)S(1)}, u32[]{:S(2)}, u32[]{:S(2)}) collective-permute-start(bf16[256,5120]{1,0:T(8,128)(2,1)S(1)} %pad_maximum_fusion), channel_id=1, source_target_pairs={{8,0},{16,8},{24,16},{0,24},{9,1},{17,9},{25,17},{1,25},{10,2},{18... | collective-permute-start | bytes 7864328 | tf_op jit(solution)/shard_map/ppermute | solution.py:57
  388.1 30.6 %collective-permute-done.25 = bf16[256,5120]{1,0:T(8,128)(2,1)S(1)} collective-permute-done((bf16[256,5120]{1,0:T(8,128)(2,1)S(1)}, bf16[256,5120]{1,0:T(8,128)(2,1)S(1)}, u32[]{:S(2)}, u32[]{:S(2)}) %collective-permute-start.25) | collective-permute-done | bytes 2621472 | tf_op jit(solution)/shard_map/ppermute | solution.py:57
  (296 shorter events, 218.5 us)
Async XLA Ops:
  9.2 78.8 %collective-permute-start = (bf16[2,64,512]{2,1,0:T(8,128)(2,1)S(1)}, bf16[2,64,512]{2,1,0:T(8,128)(2,1)S(1)}, u32[]{:S(2)}, u32[]{:S(2)}) collective-permute-start(bf16[2,64,512]{2,1,0:T(8,128)(2,1)S(1)} %get-tuple-element.226), channel_id=1, source_target_pairs={{0,1},{1,2},{2,3},{3,4},{4,5},{5,6},{6,7},{8,9},{9,10},{10,11},{11... | collective-permute-start | bytes 393224 | tf_op jit(solution)/shard_map/ppermute | solution.py:43
  13.1 74.9 %collective-permute-start.1 = (bf16[2,64,512]{2,1,0:T(8,128)(2,1)S(1)}, bf16[2,64,512]{2,1,0:T(8,128)(2,1)S(1)}, u32[]{:S(2)}, u32[]{:S(2)}) collective-permute-start(bf16[2,64,512]{2,1,0:T(8,128)(2,1)S(1)} %get-tuple-element.227), channel_id=1, source_target_pairs={{1,0},{2,1},{3,2},{4,3},{5,4},{6,5},{7,6},{9,8},{10,9},{11,10},{12... | collective-permute-start | bytes 393224 | tf_op jit(solution)/shard_map/ppermute | solution.py:44
  17.7 33.4 %all-to-all-start = ((bf16[2,8,1,64,512]{4,3,0,2,1:T(8,128)(2,1)}), bf16[2,8,1,64,512]{4,3,0,2,1:T(8,128)(2,1)}, u32[]{:S(2)}, u32[]{:S(2)}) async-start(bf16[2,8,1,64,512]{4,3,0,2,1:T(8,128)(2,1)} %fusion.51), calls=%async_computation | async-start | bytes 2097152 | tf_op jit(solution)/shard_map/all_to_all | solution.py:219
  24.1 92.8 %all-reduce.8.cloned.1.call-start = ((), (), s32[]{:S(2)}) async-start(), calls=%async_computation.4 | async-start | bytes 524288 | tf_op jit(solution)/shard_map/psum | solution.py:51
  51.2 30.9 %all-to-all-start.1 = ((bf16[2,8,1,64,512]{4,3,0,2,1:T(8,128)(2,1)}), bf16[2,8,1,64,512]{4,3,0,2,1:T(8,128)(2,1)S(1)}, u32[]{:S(2)}, u32[]{:S(2)}) async-start(bf16[2,8,1,64,512]{4,3,0,2,1:T(8,128)(2,1)} %fusion.50), calls=%async_computation.1 | async-start | bytes 2097152 | tf_op jit(solution)/shard_map/all_to_all | solution.py:219
  82.1 41.1 %all-to-all-start.2 = ((bf16[2,8,1,64,512]{4,3,0,2,1:T(8,128)(2,1)}), bf16[2,8,1,64,512]{4,3,0,2,1:T(8,128)(2,1)S(1)}, u32[]{:S(2)}, u32[]{:S(2)}) async-start(bf16[2,8,1,64,512]{4,3,0,2,1:T(8,128)(2,1)} %fusion.49), calls=%async_computation.2 | async-start | bytes 2097152 | tf_op jit(solution)/shard_map/all_to_all | solution.py:219
  86.9 288.9 %all-reduce.6.cloned.1.call-start = ((), (), s32[]{:S(2)}) async-start(), calls=%async_computation.3 | async-start | bytes 1048576 | tf_op jit(solution)/shard_map/psum | solution.py:250
  269.4 27.2 %collective-permute-start.18 = (bf16[2,1,1,64,512]{4,3,0,2,1:T(8,128)(2,1)}, bf16[2,1,1,64,512]{4,3,0,2,1:T(8,128)(2,1)}, u32[]{:S(2)}, u32[]{:S(2)}) collective-permute-start(bf16[2,1,1,64,512]{4,3,0,2,1:T(8,128)(2,1)} %get-tuple-element.207), channel_id=1, source_target_pairs={{0,1},{1,0},{2,3},{3,2},{4,5},{5,4},{6,7},{7,6},{8,9},{9,8},{10,11... | collective-permute-start | bytes 393224 | tf_op jit(solution)/shard_map/ppermute | solution.py:31
  270.7 28.1 %collective-permute-start.19 = (bf16[2,1,1,64,512]{4,3,0,2,1:T(8,128)(2,1)}, bf16[2,1,1,64,512]{4,3,0,2,1:T(8,128)(2,1)}, u32[]{:S(2)}, u32[]{:S(2)}) collective-permute-start(bf16[2,1,1,64,512]{4,3,0,2,1:T(8,128)(2,1)} %get-tuple-element.206), channel_id=1, source_target_pairs={{0,2},{1,3},{2,0},{3,1},{4,6},{5,7},{6,4},{7,5},{8,10},{9,11},{10,... | collective-permute-start | bytes 393224 | tf_op jit(solution)/shard_map/ppermute | solution.py:31
  270.7 30.1 %collective-permute-start.20 = (bf16[2,1,1,64,512]{4,3,0,2,1:T(8,128)(2,1)}, bf16[2,1,1,64,512]{4,3,0,2,1:T(8,128)(2,1)}, u32[]{:S(2)}, u32[]{:S(2)}) collective-permute-start(bf16[2,1,1,64,512]{4,3,0,2,1:T(8,128)(2,1)} %get-tuple-element.205), channel_id=1, source_target_pairs={{0,3},{1,2},{2,1},{3,0},{4,7},{5,6},{6,5},{7,4},{8,11},{9,10},{10,... | collective-permute-start | bytes 393224 | tf_op jit(solution)/shard_map/ppermute | solution.py:31
  292.0 23.5 %collective-permute-start.22 = (bf16[2,1,1,64,512]{4,3,0,2,1:T(8,128)(2,1)S(1)}, bf16[2,1,1,64,512]{4,3,0,2,1:T(8,128)(2,1)S(1)}, u32[]{:S(2)}, u32[]{:S(2)}) collective-permute-start(bf16[2,1,1,64,512]{4,3,0,2,1:T(8,128)(2,1)S(1)} %copy-done.10), channel_id=1, source_target_pairs={{0,5},{1,4},{2,7},{3,6},{4,1},{5,0},{6,3},{7,2},{8,13},{9,12},{10,... | collective-permute-start | bytes 393224 | tf_op jit(solution)/shard_map/ppermute | solution.py:31
  296.6 18.9 %collective-permute-start.23 = (bf16[2,1,1,64,512]{4,3,0,2,1:T(8,128)(2,1)S(1)}, bf16[2,1,1,64,512]{4,3,0,2,1:T(8,128)(2,1)S(1)}, u32[]{:S(2)}, u32[]{:S(2)}) collective-permute-start(bf16[2,1,1,64,512]{4,3,0,2,1:T(8,128)(2,1)S(1)} %copy-done.9), channel_id=1, source_target_pairs={{0,6},{1,7},{2,4},{3,5},{4,2},{5,3},{6,0},{7,1},{8,14},{9,15},{10,... | collective-permute-start | bytes 393224 | tf_op jit(solution)/shard_map/ppermute | solution.py:31
  298.9 19.1 %collective-permute-start.24 = (bf16[2,1,1,64,512]{4,3,0,2,1:T(8,128)(2,1)S(1)}, bf16[2,1,1,64,512]{4,3,0,2,1:T(8,128)(2,1)S(1)}, u32[]{:S(2)}, u32[]{:S(2)}) collective-permute-start(bf16[2,1,1,64,512]{4,3,0,2,1:T(8,128)(2,1)S(1)} %copy-done.8), channel_id=1, source_target_pairs={{0,7},{1,6},{2,5},{3,4},{4,3},{5,2},{6,1},{7,0},{8,15},{9,14},{10,... | collective-permute-start | bytes 393224 | tf_op jit(solution)/shard_map/ppermute | solution.py:31
  300.8 25.4 %collective-permute-start.11 = (bf16[2,1,1,64,512]{4,3,0,2,1:T(8,128)(2,1)}, bf16[2,1,1,64,512]{4,3,0,2,1:T(8,128)(2,1)}, u32[]{:S(2)}, u32[]{:S(2)}) collective-permute-start(bf16[2,1,1,64,512]{4,3,0,2,1:T(8,128)(2,1)} %get-tuple-element.214), channel_id=1, source_target_pairs={{0,1},{1,0},{2,3},{3,2},{4,5},{5,4},{6,7},{7,6},{8,9},{9,8},{10,11... | collective-permute-start | bytes 393224 | tf_op jit(solution)/shard_map/ppermute | solution.py:31
  304.0 23.9 %collective-permute-start.12 = (bf16[2,1,1,64,512]{4,3,0,2,1:T(8,128)(2,1)}, bf16[2,1,1,64,512]{4,3,0,2,1:T(8,128)(2,1)}, u32[]{:S(2)}, u32[]{:S(2)}) collective-permute-start(bf16[2,1,1,64,512]{4,3,0,2,1:T(8,128)(2,1)} %get-tuple-element.213), channel_id=1, source_target_pairs={{0,2},{1,3},{2,0},{3,1},{4,6},{5,7},{6,4},{7,5},{8,10},{9,11},{10,... | collective-permute-start | bytes 393224 | tf_op jit(solution)/shard_map/ppermute | solution.py:31
  315.5 18.5 %collective-permute-start.13 = (bf16[2,1,1,64,512]{4,3,0,2,1:T(8,128)(2,1)}, bf16[2,1,1,64,512]{4,3,0,2,1:T(8,128)(2,1)}, u32[]{:S(2)}, u32[]{:S(2)}) collective-permute-start(bf16[2,1,1,64,512]{4,3,0,2,1:T(8,128)(2,1)} %get-tuple-element.212), channel_id=1, source_target_pairs={{0,3},{1,2},{2,1},{3,0},{4,7},{5,6},{6,5},{7,4},{8,11},{9,10},{10,... | collective-permute-start | bytes 393224 | tf_op jit(solution)/shard_map/ppermute | solution.py:31
  315.5 20.0 %collective-permute-start.14 = (bf16[2,1,1,64,512]{4,3,0,2,1:T(8,128)(2,1)}, bf16[2,1,1,64,512]{4,3,0,2,1:T(8,128)(2,1)}, u32[]{:S(2)}, u32[]{:S(2)}) collective-permute-start(bf16[2,1,1,64,512]{4,3,0,2,1:T(8,128)(2,1)} %get-tuple-element.211), channel_id=1, source_target_pairs={{0,4},{1,5},{2,6},{3,7},{4,0},{5,1},{6,2},{7,3},{8,12},{9,13},{10,... | collective-permute-start | bytes 393224 | tf_op jit(solution)/shard_map/ppermute | solution.py:31
  318.0 22.4 %collective-permute-start.15 = (bf16[2,1,1,64,512]{4,3,0,2,1:T(8,128)(2,1)}, bf16[2,1,1,64,512]{4,3,0,2,1:T(8,128)(2,1)}, u32[]{:S(2)}, u32[]{:S(2)}) collective-permute-start(bf16[2,1,1,64,512]{4,3,0,2,1:T(8,128)(2,1)} %get-tuple-element.210), channel_id=1, source_target_pairs={{0,5},{1,4},{2,7},{3,6},{4,1},{5,0},{6,3},{7,2},{8,13},{9,12},{10,... | collective-permute-start | bytes 393224 | tf_op jit(solution)/shard_map/ppermute | solution.py:31
  333.9 16.6 %collective-permute-start.4 = (bf16[2,1,1,64,512]{4,3,0,2,1:T(8,128)(2,1)}, bf16[2,1,1,64,512]{4,3,0,2,1:T(8,128)(2,1)}, u32[]{:S(2)}, u32[]{:S(2)}) collective-permute-start(bf16[2,1,1,64,512]{4,3,0,2,1:T(8,128)(2,1)} %get-tuple-element.221), channel_id=1, source_target_pairs={{0,1},{1,0},{2,3},{3,2},{4,5},{5,4},{6,7},{7,6},{8,9},{9,8},{10,11... | collective-permute-start | bytes 393224 | tf_op jit(solution)/shard_map/ppermute | solution.py:31
  335.5 16.8 %collective-permute-start.5 = (bf16[2,1,1,64,512]{4,3,0,2,1:T(8,128)(2,1)}, bf16[2,1,1,64,512]{4,3,0,2,1:T(8,128)(2,1)}, u32[]{:S(2)}, u32[]{:S(2)}) collective-permute-start(bf16[2,1,1,64,512]{4,3,0,2,1:T(8,128)(2,1)} %get-tuple-element.220), channel_id=1, source_target_pairs={{0,2},{1,3},{2,0},{3,1},{4,6},{5,7},{6,4},{7,5},{8,10},{9,11},{10,... | collective-permute-start | bytes 393224 | tf_op jit(solution)/shard_map/ppermute | solution.py:31
  340.4 17.5 %collective-permute-start.6 = (bf16[2,1,1,64,512]{4,3,0,2,1:T(8,128)(2,1)}, bf16[2,1,1,64,512]{4,3,0,2,1:T(8,128)(2,1)}, u32[]{:S(2)}, u32[]{:S(2)}) collective-permute-start(bf16[2,1,1,64,512]{4,3,0,2,1:T(8,128)(2,1)} %get-tuple-element.219), channel_id=1, source_target_pairs={{0,3},{1,2},{2,1},{3,0},{4,7},{5,6},{6,5},{7,4},{8,11},{9,10},{10,... | collective-permute-start | bytes 393224 | tf_op jit(solution)/shard_map/ppermute | solution.py:31
  342.0 17.5 %collective-permute-start.7 = (bf16[2,1,1,64,512]{4,3,0,2,1:T(8,128)(2,1)}, bf16[2,1,1,64,512]{4,3,0,2,1:T(8,128)(2,1)}, u32[]{:S(2)}, u32[]{:S(2)}) collective-permute-start(bf16[2,1,1,64,512]{4,3,0,2,1:T(8,128)(2,1)} %get-tuple-element.218), channel_id=1, source_target_pairs={{0,4},{1,5},{2,6},{3,7},{4,0},{5,1},{6,2},{7,3},{8,12},{9,13},{10,... | collective-permute-start | bytes 393224 | tf_op jit(solution)/shard_map/ppermute | solution.py:31
  343.3 18.3 %collective-permute-start.8 = (bf16[2,1,1,64,512]{4,3,0,2,1:T(8,128)(2,1)}, bf16[2,1,1,64,512]{4,3,0,2,1:T(8,128)(2,1)}, u32[]{:S(2)}, u32[]{:S(2)}) collective-permute-start(bf16[2,1,1,64,512]{4,3,0,2,1:T(8,128)(2,1)} %get-tuple-element.217), channel_id=1, source_target_pairs={{0,5},{1,4},{2,7},{3,6},{4,1},{5,0},{6,3},{7,2},{8,13},{9,12},{10,... | collective-permute-start | bytes 393224 | tf_op jit(solution)/shard_map/ppermute | solution.py:31
  382.8 36.0 %collective-permute-start.25 = (bf16[256,5120]{1,0:T(8,128)(2,1)S(1)}, bf16[256,5120]{1,0:T(8,128)(2,1)S(1)}, u32[]{:S(2)}, u32[]{:S(2)}) collective-permute-start(bf16[256,5120]{1,0:T(8,128)(2,1)S(1)} %pad_maximum_fusion), channel_id=1, source_target_pairs={{8,0},{16,8},{24,16},{0,24},{9,1},{17,9},{25,17},{1,25},{10,2},{18... | collective-permute-start | bytes 7864328 | tf_op jit(solution)/shard_map/ppermute | solution.py:57
  (39 other events, 452.9 us)
Sparse Core Ops, SparseCore 0:
  30.9 86.0 all-reduce.7
  279.7 95.4 all-reduce.5
